TPU v7x, 512 devices: a whole 4x4x16 slice. The times are simulated.
512 devices in a mesh: row: 64 (over z, x), rep: 8 (over y, core).
Axes of the slice: x: 4, y: 4, z: 16, core: 2. Of those that a mesh axis runs over, the one named last changes fastest.
Arguments:
- features: bfloat16 [16384, 128], P('row', 'rep'), may hold values from -6 to 6
- owner_index: int32 [16384], P('row'), may hold values from 0 to 16383, as said below
- block_cols: int32 [128, 64], P('row', 'rep'), may hold values from 0 to 127, as said below
- block_count: int32 [128], P('row'), may hold values from 1 to 64, as said below
- tiles: bfloat16 [128, 64, 128, 128], P('row', 'rep'), may hold values from -0.109375 to 0.109375
- weight: bfloat16 [128, 256], P(None, 'rep'), may hold values from -0.75 to 0.75
- bias: float32 [256], P('rep'), may hold values from -4 to 4
- grad_out: bfloat16 [16384, 256], P('row', 'rep'), may hold values from -6 to 6
Outputs:
- hidden: bfloat16 [16384, 256], P('row', 'rep')
- weight_grad: float32 [128, 256], P(None, 'rep')
- bias_grad: float32 [256], P('rep')
Inputs may be any that keep to these rules, and one draw needn't show every extreme that they name: `owner_index`: A permutation; the 256 rows of each loader shard hold exactly 4 positions of every partition's 2*128 rows. `block_cols`: the block columns of one block row are distinct. Block column c belongs to partition c // 2. Over all slots of one partition's 2 block rows, exactly 1 distinct block columns of each partition are named. `block_count`: some block row has all 64 slots live.
All inputs are finite; a program needn't handle non-finite values.
Results may differ from a plain program's by a relative error of at most 0.017.
Values may be sent and summed in bfloat16 or wider, within the bound.
No kernel may reach another device: no remote copies, remote signals or barrier semaphores. Data moves between devices by JAX's collectives and lax.ppermute only.
A program may use at most 64 MiB of HBM per device.

v0:
```python
import jax
import jax.numpy as jnp
from jax import lax
from jax.sharding import PartitionSpec as P


def block_product(tile_set, col_set, live, table, rows_part):
    size_blk = tile_set.shape[2]
    width = table.shape[1]
    blocks = table.reshape(table.shape[0] // size_blk, size_blk, width)
    picked = blocks[col_set]
    picked = jnp.where(live[:, :, None, None], picked, jnp.zeros_like(picked))
    summed = jnp.einsum("rkij,rkjc->ric", tile_set, picked, preferred_element_type=jnp.float32)
    return summed.reshape(rows_part, width)


def on_device(features, owner_index, block_cols, block_count, tiles, weight, bias, grad_out):
    rows_part = features.shape[0]
    cols_dev = features.shape[1]
    parts_count = lax.axis_size("row")
    per_pair = rows_part // parts_count
    destination = owner_index // rows_part
    order = jnp.argsort(destination, stable=True)
    send_rows = features[order].reshape(parts_count, per_pair, cols_dev)
    send_pos = (owner_index[order] % rows_part).reshape(parts_count, per_pair)
    got_rows, got_pos = (
        lax.all_to_all(send_rows, "row", split_axis=0, concat_axis=0, tiled=True),
        lax.all_to_all(send_pos, "row", split_axis=0, concat_axis=0, tiled=True),
    )
    owned = (
        jnp.zeros((rows_part, cols_dev), jnp.bfloat16)
        .at[got_pos.reshape(rows_part)]
        .set(got_rows.reshape(rows_part, cols_dev))
    )
    wide_own = lax.all_gather(owned, "rep", axis=1, tiled=True)
    table = lax.all_gather(wide_own, "row", axis=0, tiled=True)
    slots_dev = block_cols.shape[1]
    slot_ids = lax.axis_index("rep") * slots_dev + jnp.arange(slots_dev, dtype=jnp.int32)
    live = slot_ids[None, :] < block_count[:, None]
    partial_agg = block_product(tiles, block_cols, live, table, rows_part)
    agg = lax.psum(partial_agg.astype(jnp.bfloat16), "rep")
    pre = jnp.dot(agg, weight, preferred_element_type=jnp.float32) + bias
    hidden = jax.nn.silu(pre).astype(jnp.bfloat16)
    sig = jax.nn.sigmoid(pre)
    dpre = (grad_out.astype(jnp.float32) * sig * (1.0 + pre * (1.0 - sig))).astype(jnp.bfloat16)
    weight_term = jnp.dot(agg.T, dpre, preferred_element_type=jnp.float32)
    bias_term = jnp.sum(dpre.astype(jnp.float32), axis=0)
    weight_grad, bias_grad = lax.psum((weight_term, bias_term), "row")
    return (hidden, weight_grad, bias_grad)


def solution(mesh):
    placed = (
        P("row", "rep"),
        P("row"),
        P("row", "rep"),
        P("row"),
        P("row", "rep", None, None),
        P(None, "rep"),
        P("rep"),
        P("row", "rep"),
    )
    return jax.shard_map(
        on_device,
        mesh=mesh,
        in_specs=placed,
        out_specs=(P("row", "rep"), P(None, "rep"), P("rep")),
        check_vma=False,
    )
```

profile of v0, /device:TPU:8, one launch (start us, length us, event | category | flops | bytes accessed | tf_op | source)
XLA Modules:
  0.0 583.7 jit_solution(2200357898452502559)
XLA Ops:
  7.2 0.7 and_select_fusion
  7.9 3.2 sort.17
  11.1 2.0 gather_fusion
  13.2 0.6 add_select_fusion
  13.8 18.6 %all-to-all-start = ((s32[64,1,4]{2,1,0:T(1,128)}), s32[64,1,4]{2,1,0:T(1,128)S(1)}, u32[]{:S(2)}, u32[]{:S(2)}) async-start(s32[64,1,4]{2,1,0:T(1,128)} %bitcast), calls=%async_computation | async-start | bytes 65536 | tf_op jit(solution)/shard_map/all_to_all | solution.py:28
  32.4 0.8 copy.18
  33.2 1.5 gather_fusion.1
  34.7 12.5 %all-to-all-done = s32[64,1,4]{2,1,0:T(1,128)S(1)} async-done(((s32[64,1,4]{2,1,0:T(1,128)}), s32[64,1,4]{2,1,0:T(1,128)S(1)}, u32[]{:S(2)}, u32[]{:S(2)}) %all-to-all-start) | async-done | bytes 1056 | tf_op jit(solution)/shard_map/all_to_all | solution.py:28
  47.2 4.6 all-to-all-start.1
  51.8 0.5 broadcast.122
  52.3 0.7 reduce.3
  53.2 13.9 %all-to-all-done.1 = bf16[64,4,16]{2,1,0:T(4,128)(2,1)S(1)} async-done(((bf16[64,4,16]{2,1,0:T(4,128)(2,1)}), bf16[64,4,16]{2,1,0:T(4,128)(2,1)S(1)}, u32[]{:S(2)}, u32[]{:S(2)}) %all-to-all-start.1) | async-done | bytes 8224 | tf_op jit(solution)/shard_map/all_to_all | solution.py:27
  67.1 1.2 scatter_custom_fusion
  68.3 14.0 %all_gather.6 = bf16[256,128]{0,1:T(8,128)(2,1)} all-gather(bf16[256,16]{0,1:T(8,128)(2,1)S(1)} %copy.19), channel_id=1, replica_groups=mesh['row'=64,'rep'=8] {'rep'}, dimensions={1}, use_global_device_ids=true | all-gather | bytes 73728 | tf_op jit(solution)/shard_map/all_gather | solution.py:35
  82.4 0.7 compare_select_fusion.1
  83.2 0.7 broadcast_compare_fusion
  83.9 133.4 %all-gather.2.cloned.1.call-done = bf16[16384,128]{0,1:T(8,128)(2,1)} async-done(((bf16[256,128]{0,1:T(8,128)(2,1)}), bf16[16384,128]{0,1:T(8,128)(2,1)}) %all-gather.2.cloned.1.call-update) | async-done | bytes 4194320 | tf_op jit(solution)/shard_map/all_gather | solution.py:36
  217.4 6.4 %copy.20 = bf16[16384,128]{1,0:T(8,128)(2,1)} copy(bf16[16384,128]{0,1:T(8,128)(2,1)} %all-gather.2.cloned.1.call-done) | data formatting | bytes 8388608 | tf_op jit(solution)/shard_map/all_gather | solution.py:36
  223.7 2.8 gather_fusion.2
  226.6 1.0 fusion
  227.6 66.4 %all-reduce.3.cloned.1.call-done = bf16[256,128]{1,0:T(8,128)(2,1)} async-done(((bf16[256,128]{1,0:T(8,128)(2,1)}), bf16[256,128]{1,0:T(8,128)(2,1)}) %all-reduce.3.cloned.1.call-update) | async-done | bytes 65552 | tf_op jit(solution)/shard_map/psum | solution.py:41
  294.0 1.7 convert_reduce_fusion
  295.8 1.0 fusion.8
  296.7 280.1 %all-reduce = (f32[128,32]{0,1:T(8,128)}, f32[32]{0:T(128)}) all-reduce(f32[128,32]{0,1:T(8,128)S(1)} %fusion.8, f32[32]{0:T(128)S(1)} %get-tuple-element.7), channel_id=1, replica_groups=mesh['row'=64,'rep'=8] {'row'}, use_global_device_ids=true, to_apply=%region_3.4 | all-reduce | flops 4128 | bytes 33024 | tf_op jit(solution)/shard_map/psum | solution.py:48
  (22 shorter events, 0.5 us)
Async XLA Ops:
  7.2 219.4 %copy-start = (bf16[2,8,128,128]{3,2,1,0:T(8,128)(2,1)S(1)}, bf16[2,8,128,128]{3,2,1,0:T(8,128)(2,1)}, u32[]{:S(2)}) copy-start(bf16[2,8,128,128]{3,2,1,0:T(8,128)(2,1)} %param.12) | copy-start | bytes 1572868
  13.8 33.3 %all-to-all-start = ((s32[64,1,4]{2,1,0:T(1,128)}), s32[64,1,4]{2,1,0:T(1,128)S(1)}, u32[]{:S(2)}, u32[]{:S(2)}) async-start(s32[64,1,4]{2,1,0:T(1,128)} %bitcast), calls=%async_computation | async-start | bytes 65536 | tf_op jit(solution)/shard_map/all_to_all | solution.py:28
  47.2 19.9 %all-to-all-start.1 = ((bf16[64,4,16]{2,1,0:T(4,128)(2,1)}), bf16[64,4,16]{2,1,0:T(4,128)(2,1)S(1)}, u32[]{:S(2)}, u32[]{:S(2)}) async-start(bf16[64,4,16]{2,1,0:T(4,128)(2,1)} %bitcast.2), calls=%async_computation.1 | async-start | bytes 131072 | tf_op jit(solution)/shard_map/all_to_all | solution.py:27
  51.8 165.6 %all-gather.2.cloned.1.call-start = ((), (), s32[]{:S(2)}) async-start(), calls=%async_computation.2 | async-start | bytes 4259840 | tf_op jit(solution)/shard_map/all_gather | solution.py:36
  82.4 211.7 %all-reduce.3.cloned.1.call-start = ((), (), s32[]{:S(2)}) async-start(), calls=%async_computation.3 | async-start | bytes 131072 | tf_op jit(solution)/shard_map/psum | solution.py:41
  83.9 210.1 %copy-start.1 = (bf16[256,32]{0,1:T(8,128)(2,1)S(1)}, bf16[256,32]{0,1:T(8,128)(2,1)}, u32[]{:S(2)}) copy-start(bf16[256,32]{0,1:T(8,128)(2,1)} %param.15) | copy-start | bytes 49156
  83.9 210.1 %copy-start.2 = (bf16[128,32]{0,1:T(8,128)(2,1)S(1)}, bf16[128,32]{0,1:T(8,128)(2,1)}, u32[]{:S(2)}) copy-start(bf16[128,32]{0,1:T(8,128)(2,1)} %param.13) | copy-start | bytes 24580
  83.9 210.1 %copy-start.3 = (f32[32]{0:T(128)S(1)}, f32[32]{0:T(128)}, u32[]{:S(2)}) copy-start(f32[32]{0:T(128)} %param.14) | copy-start | bytes 388
Sparse Core Ops, SparseCore 0:
  82.5 134.8 all-gather.1
  227.7 66.2 all-reduce.2
where the time goes:
time: 584 us
  blocking collectives  294 us (50%)
  waiting for transfers between devices  226 us (39%)
  starting transfers between devices  23.3 us (4%)
  local copies, waits for them, and re-layouts  15.5 us (3%)
  between operations  14.1 us (2%)
  other arithmetic  6.69 us (1%)
    psum x1, blocking collectives, on_device(): weight_grad, bias_grad = lax.psum((weight_term, bias_term), 'row')  280 us
    all_gather x1, waiting for transfers between devices, on_device(): table = lax.all_gather(wide_own, 'row', axis=0, tiled=True)  133 us
    psum x1, waiting for transfers between devices, on_device(): agg = lax.psum(partial_agg.astype(jnp.bfloat16), 'rep')  66.4 us
    all_to_all x1, starting transfers between devices, on_device(): lax.all_to_all(send_pos, 'row', split_axis=0, concat_axis=0, tiled=True)  18.6 us
    all_gather x1, blocking collectives, on_device(): wide_own = lax.all_gather(owned, 'rep', axis=1, tiled=True)  14 us
    all_to_all x1, waiting for transfers between devices, on_device(): lax.all_to_all(send_rows, 'row', split_axis=0, concat_axis=0, tiled=True)  13.9 us
    all_to_all x1, waiting for transfers between devices, on_device(): lax.all_to_all(send_pos, 'row', split_axis=0, concat_axis=0, tiled=True)  12.5 us
  transfers between devices with their start and end apart: 4, of which 4 were waited for; matrix products, arithmetic and copies ran while one was open for 1% of the time, Pallas kernels for 0%

commit v1 on v0

--- a/solution.py
+++ b/solution.py
@@ -2,6 +2,12 @@
 import jax.numpy as jnp
 from jax import lax
 from jax.sharding import PartitionSpec as P
+
+
+def laid_out(blocks, dim):
+    shape = list(blocks.shape[1:])
+    shape[dim] *= blocks.shape[0]
+    return jnp.moveaxis(blocks, 0, dim).reshape(shape)
 
 
 def block_product(tile_set, col_set, live, table, rows_part):
@@ -32,7 +38,19 @@
         .at[got_pos.reshape(rows_part)]
         .set(got_rows.reshape(rows_part, cols_dev))
     )
-    wide_own = lax.all_gather(owned, "rep", axis=1, tiled=True)
+    count = lax.axis_size("rep")
+    pairs = [(i, (i + 1) % count) for i in range(count)]
+    back = [(b, a) for a, b in pairs]
+    lower, upper = ([], [])
+    for step in range(count - 1):
+        if step % 2 == 0:
+            lower.append(lax.ppermute(lower[-1] if lower else owned, "rep", pairs))
+        else:
+            upper.append(lax.ppermute(upper[-1] if upper else owned, "rep", back))
+    pieces = jnp.stack([*lower[::-1], owned, *upper])
+    shift = lax.axis_index("rep") - len(lower)
+    pieces = pieces[(jnp.arange(count) - shift) % count]
+    wide_own = laid_out(pieces, 1)
     table = lax.all_gather(wide_own, "row", axis=0, tiled=True)
     slots_dev = block_cols.shape[1]
     slot_ids = lax.axis_index("rep") * slots_dev + jnp.arange(slots_dev, dtype=jnp.int32)

time: 584 us -> 589 us (level)
  blocking collectives: 294 us -> 280 us
  waiting for transfers between devices: 226 us -> 238 us
    all_gather x1 -> x0, blocking collectives: 14 us -> none  [on_device(): wide_own = lax.all_gather(owned, 'rep', axis=1, tiled=True)]
    ppermute x0 -> x7, waiting for transfers between devices: none -> 8.66 us  [the longest x4 8.65 us: on_device(): lower.append(lax.ppermute(lower[-1] if lower else owned, 'rep', pairs))]
  transfers between devices with their start and end apart: 4 -> 11, of which waited for: 4 -> 8; matrix products, arithmetic and copies ran while one was open for 1% -> 1% of each run, Pallas kernels for 0% -> 0%
where the time goes in v1:
time: 589 us; the launch traced here: 588 us
  blocking collectives  280 us (48%)
  waiting for transfers between devices  238 us (40%)
  starting transfers between devices  28.8 us (5%)
  local copies, waits for them, and re-layouts  17.3 us (3%)
  between operations  14.2 us (2%)
  other arithmetic  6.71 us (1%)
    psum x1, blocking collectives, on_device(): weight_grad, bias_grad = lax.psum((weight_term, bias_term), 'row')  280 us
    all_gather x1, waiting for transfers between devices, on_device(): table = lax.all_gather(wide_own, 'row', axis=0, tiled=True)  136 us
    psum x1, waiting for transfers between devices, on_device(): agg = lax.psum(partial_agg.astype(jnp.bfloat16), 'rep')  66.4 us
    all_to_all x1, starting transfers between devices, on_device(): lax.all_to_all(send_pos, 'row', split_axis=0, concat_axis=0, tiled=True)  18.6 us
    all_to_all x1, waiting for transfers between devices, on_device(): lax.all_to_all(send_rows, 'row', split_axis=0, concat_axis=0, tiled=True)  13.9 us
    all_to_all x1, waiting for transfers between devices, on_device(): lax.all_to_all(send_pos, 'row', split_axis=0, concat_axis=0, tiled=True)  12.5 us
  transfers between devices with their start and end apart: 11, of which 8 were waited for; matrix products, arithmetic and copies ran while one was open for 1% of the time, Pallas kernels for 0%

profile of v1, /device:TPU:8, one launch (start us, length us, event | category | flops | bytes accessed | tf_op | source)
XLA Modules:
  0.0 588.3 jit_solution(14362353342627015613)
XLA Ops:
  7.9 3.2 sort.17
  11.1 2.0 gather_fusion
  13.9 18.6 %all-to-all-start = ((s32[64,1,4]{2,1,0:T(1,128)}), s32[64,1,4]{2,1,0:T(1,128)S(1)}, u32[]{:S(2)}, u32[]{:S(2)}) async-start(s32[64,1,4]{2,1,0:T(1,128)} %bitcast), calls=%async_computation | async-start | bytes 65536 | tf_op jit(solution)/shard_map/all_to_all | solution.py:34
  33.2 1.5 gather_fusion.1
  34.7 12.5 %all-to-all-done = s32[64,1,4]{2,1,0:T(1,128)S(1)} async-done(((s32[64,1,4]{2,1,0:T(1,128)}), s32[64,1,4]{2,1,0:T(1,128)S(1)}, u32[]{:S(2)}, u32[]{:S(2)}) %all-to-all-start) | async-done | bytes 1056 | tf_op jit(solution)/shard_map/all_to_all | solution.py:34
  47.2 4.6 all-to-all-start.1
  53.2 13.9 %all-to-all-done.1 = bf16[64,4,16]{2,1,0:T(4,128)(2,1)S(1)} async-done(((bf16[64,4,16]{2,1,0:T(4,128)(2,1)}), bf16[64,4,16]{2,1,0:T(4,128)(2,1)S(1)}, u32[]{:S(2)}, u32[]{:S(2)}) %all-to-all-start.1) | async-done | bytes 8224 | tf_op jit(solution)/shard_map/all_to_all | solution.py:33
  67.1 1.2 scatter_custom_fusion
  68.3 1.7 collective-permute-start.4
  70.0 1.9 collective-permute-done
  72.0 1.7 collective-permute-start.5
  73.7 1.9 collective-permute-done.1
  75.7 2.0 collective-permute-start.6
  77.7 1.6 collective-permute-done.2
  79.9 3.1 collective-permute-done.3
  83.2 1.2 gather_fusion.2
  86.0 136.0 %all-gather.2.cloned.1.call-done = bf16[16384,128]{0,1:T(8,128)(2,1)} async-done(((bf16[256,128]{0,1:T(8,128)(2,1)}), bf16[16384,128]{0,1:T(8,128)(2,1)}) %all-gather.2.cloned.1.call-update) | async-done | bytes 4194320 | tf_op jit(solution)/shard_map/all_gather | solution.py:54
  222.0 6.4 %copy.30 = bf16[16384,128]{1,0:T(8,128)(2,1)} copy(bf16[16384,128]{0,1:T(8,128)(2,1)} %all-gather.2.cloned.1.call-done) | data formatting | bytes 8388608 | tf_op jit(solution)/shard_map/all_gather | solution.py:54
  228.4 2.8 gather_fusion.3
  231.2 1.0 fusion
  232.2 66.4 %all-reduce.3.cloned.1.call-done = bf16[256,128]{1,0:T(8,128)(2,1)} async-done(((bf16[256,128]{1,0:T(8,128)(2,1)}), bf16[256,128]{1,0:T(8,128)(2,1)}) %all-reduce.3.cloned.1.call-update) | async-done | bytes 65552 | tf_op jit(solution)/shard_map/psum | solution.py:59
  298.7 1.7 convert_reduce_fusion
  300.4 1.0 fusion.10
  301.4 280.1 %all-reduce = (f32[128,32]{0,1:T(8,128)}, f32[32]{0:T(128)}) all-reduce(f32[128,32]{0,1:T(8,128)S(1)} %fusion.10, f32[32]{0:T(128)S(1)} %get-tuple-element.7), channel_id=1, replica_groups=mesh['row'=64,'rep'=8] {'row'}, use_global_device_ids=true, to_apply=%region_3.4 | all-reduce | flops 4128 | bytes 33024 | tf_op jit(solution)/shard_map/psum | solution.py:66
  (52 shorter events, 6.0 us)
Async XLA Ops:
  7.2 224.1 %copy-start = (bf16[2,8,128,128]{3,2,1,0:T(8,128)(2,1)S(1)}, bf16[2,8,128,128]{3,2,1,0:T(8,128)(2,1)}, u32[]{:S(2)}) copy-start(bf16[2,8,128,128]{3,2,1,0:T(8,128)(2,1)} %param.12) | copy-start | bytes 1572868
  13.9 33.3 %all-to-all-start = ((s32[64,1,4]{2,1,0:T(1,128)}), s32[64,1,4]{2,1,0:T(1,128)S(1)}, u32[]{:S(2)}, u32[]{:S(2)}) async-start(s32[64,1,4]{2,1,0:T(1,128)} %bitcast), calls=%async_computation | async-start | bytes 65536 | tf_op jit(solution)/shard_map/all_to_all | solution.py:34
  47.2 19.9 %all-to-all-start.1 = ((bf16[64,4,16]{2,1,0:T(4,128)(2,1)}), bf16[64,4,16]{2,1,0:T(4,128)(2,1)S(1)}, u32[]{:S(2)}, u32[]{:S(2)}) async-start(bf16[64,4,16]{2,1,0:T(4,128)(2,1)} %bitcast.2), calls=%async_computation.1 | async-start | bytes 131072 | tf_op jit(solution)/shard_map/all_to_all | solution.py:33
  51.8 170.2 %all-gather.2.cloned.1.call-start = ((), (), s32[]{:S(2)}) async-start(), calls=%async_computation.2 | async-start | bytes 4259840 | tf_op jit(solution)/shard_map/all_gather | solution.py:54
  68.3 3.7 collective-permute-start
  68.3 3.7 collective-permute-start.4
  72.0 3.7 collective-permute-start.1
  72.0 3.7 collective-permute-start.5
  75.7 3.7 collective-permute-start.2
  75.7 4.2 collective-permute-start.6
  79.4 3.7 collective-permute-start.3
  84.4 214.3 %all-reduce.3.cloned.1.call-start = ((), (), s32[]{:S(2)}) async-start(), calls=%async_computation.3 | async-start | bytes 131072 | tf_op jit(solution)/shard_map/psum | solution.py:59
  85.9 212.7 %copy-start.1 = (bf16[256,32]{0,1:T(8,128)(2,1)S(1)}, bf16[256,32]{0,1:T(8,128)(2,1)}, u32[]{:S(2)}) copy-start(bf16[256,32]{0,1:T(8,128)(2,1)} %param.15) | copy-start | bytes 49156
  85.9 212.7 %copy-start.2 = (bf16[128,32]{0,1:T(8,128)(2,1)S(1)}, bf16[128,32]{0,1:T(8,128)(2,1)}, u32[]{:S(2)}) copy-start(bf16[128,32]{0,1:T(8,128)(2,1)} %param.13) | copy-start | bytes 24580
  85.9 212.7 %copy-start.3 = (f32[32]{0:T(128)S(1)}, f32[32]{0:T(128)}, u32[]{:S(2)}) copy-start(f32[32]{0:T(128)} %param.14) | copy-start | bytes 388
Sparse Core Ops, SparseCore 0:
  84.5 137.4 all-gather.1
  232.4 66.2 all-reduce.2
